TPU v7x, 32 devices: a whole 2x2x4 slice. The times are simulated.
32 devices in a mesh: layer: 4 (over y, x), tok: 8 (over z, core).
Axes of the slice: x: 2, y: 2, z: 4, core: 2. Of those that a mesh axis runs over, the one named last changes fastest.
Arguments:
- residual: bfloat16 [4, 1024, 3584], P('layer', 'tok'), may hold values from -6 to 6
- targets: bfloat16 [4, 1024, 3584], P('layer', 'tok'), may hold values from -6 to 6
- block_ids: int32 [4, 1024, 2], P(None, 'tok'), may hold values from 0 to 127, all different within a row; in each aligned block of 128 rows (0 to 127, 128 to 255, ..., all dimensions but the last counted through in order) at most 4 rows name the same one
- encoder_weight: bfloat16 [4, 3584, 16384], P('layer', None, 'tok'), may hold values from -0.09375 to 0.09375
- encoder_bias: float32 [4, 16384], P('layer', 'tok'), may hold values from -3 to 3
- decoder_weight: bfloat16 [4, 4, 16384, 3584], P('layer', None, 'tok'), may hold values from -0.25 to 0.25
- decoder_bias: float32 [4, 3584], P('layer'), may hold values from -3 to 3
Outputs:
- reconstruction: bfloat16 [4, 1024, 3584], P('layer', 'tok')
- error: float32 [4, 1024], P('layer', 'tok')
Inputs may be any that keep to these rules, and one draw needn't show every extreme that they name: `block_ids`: A token's 2 blocks in a layer are distinct. In each layer, the 128 rows of one device (aligned blocks of tokens) name no block more than 4 times, and some block exactly 4 times.
All inputs are finite; a program needn't handle non-finite values.
Results may differ from a plain program's by a relative error of at most 0.0053.
Values may be sent and summed in bfloat16 or wider, within the bound.
No kernel may reach another device: no remote copies, remote signals or barrier semaphores. Data moves between devices by JAX's collectives and lax.ppermute only.
A program may use at most 192 MiB of HBM per device.

v0:
```python
import jax
import jax.numpy as jnp
from jax import lax
from jax.sharding import PartitionSpec as P

BLOCK = 128


def slot_positions(ids, blocks, capacity):
    flat_ids = ids.reshape(-1)
    onehot = (flat_ids[:, None] == jnp.arange(blocks, dtype=jnp.int32)[None, :]).astype(jnp.int32)
    before = jnp.cumsum(onehot, axis=0) - onehot
    rank_in = jnp.sum(before * onehot, axis=1)
    return flat_ids * capacity + rank_in


def body(residual, targets, block_ids, encoder_weight, encoder_bias, decoder_weight, decoder_bias):
    layer_index = lax.axis_index("layer")
    layers = lax.axis_size("layer")
    tok_count = lax.axis_size("tok")
    tok_rows = residual.shape[1]
    width = residual.shape[2]
    topk = block_ids.shape[2]
    per_owner = encoder_weight.shape[2] // BLOCK
    blocks = per_owner * tok_count
    capacity = max(2, 2 * tok_rows * topk // blocks)
    slot_count = blocks * capacity
    positions = jax.vmap(lambda ids: slot_positions(ids, blocks, capacity))(block_ids)
    own_positions = lax.dynamic_index_in_dim(positions, layer_index, 0, keepdims=False)
    source_row = (
        jnp.full((slot_count,), tok_rows, jnp.int32)
        .at[own_positions]
        .set(jnp.arange(tok_rows * topk, dtype=jnp.int32) // topk)
    )
    padded = jnp.concatenate([residual[0], jnp.zeros((1, width), residual.dtype)], axis=0)
    outgoing = padded[source_row].reshape(tok_count, per_owner * capacity, width)
    arrived = lax.all_to_all(outgoing, "tok", split_axis=0, concat_axis=0, tiled=True)
    arrived = arrived.reshape(tok_count, per_owner, capacity, width)
    enc_blocks = encoder_weight[0].reshape(width, per_owner, BLOCK)
    pre = jnp.einsum("sbcd,dbe->sbce", arrived, enc_blocks, preferred_element_type=jnp.float32)
    pre = pre + encoder_bias[0].reshape(per_owner, BLOCK)[None, :, None, :]
    codes = (
        jnp.maximum(pre, 0.0)
        .astype(jnp.bfloat16)
        .reshape(1, tok_count, per_owner * capacity, BLOCK)
    )
    all_codes = lax.all_gather(codes, "layer", axis=0, tiled=True)
    sources = jnp.arange(layers, dtype=jnp.int32)
    valid = sources <= layer_index
    weights = decoder_weight[0]
    keep_slot = valid.astype(jnp.float32)
    slot_sets = sources.shape[0]
    chosen_codes = (
        jnp.take(all_codes, sources, axis=0) * valid.astype(jnp.bfloat16)[:, None, None, None]
    )
    terms = (
        jnp.einsum(
            "snbce,sbed->snbcd",
            chosen_codes.reshape(slot_sets, tok_count, per_owner, capacity, BLOCK),
            weights.reshape(slot_sets, per_owner, BLOCK, width),
            preferred_element_type=jnp.float32,
        )
        .astype(jnp.bfloat16)
        .reshape(slot_sets, tok_count, per_owner * capacity, width)
    )
    returned = lax.all_to_all(terms, "tok", split_axis=1, concat_axis=1, tiled=True).reshape(
        slot_sets, slot_count, width
    )
    source_positions = jnp.take(positions, sources, axis=0)
    picked = jax.vmap(lambda rows, where_at: rows[where_at])(returned, source_positions)
    parts = jnp.sum(picked.astype(jnp.float32).reshape(slot_sets, tok_rows, topk, width), axis=2)
    own_sum = jnp.sum(parts * keep_slot[:, None, None], axis=0)
    recon32 = decoder_bias[0][None, :] + own_sum
    difference = recon32 - targets[0].astype(jnp.float32)
    error = jnp.mean(difference * difference, axis=1)
    return (recon32.astype(jnp.bfloat16)[None], error[None])


def solution(mesh):
    in_specs = (
        P("layer", "tok", None),
        P("layer", "tok", None),
        P(None, "tok", None),
        P("layer", None, "tok"),
        P("layer", "tok"),
        P("layer", None, "tok", None),
        P("layer", None),
    )
    out_specs = (P("layer", "tok", None), P("layer", "tok"))
    return jax.shard_map(body, mesh=mesh, in_specs=in_specs, out_specs=out_specs, check_vma=False)
```

profile of v0, /device:TPU:0, one launch (start us, length us, event | category | flops | bytes accessed | tf_op | source)
XLA Modules:
  0.0 584.5 jit_solution(2805510803366540468)
XLA Ops:
  0.6 0.8 copy.34
  1.5 1.0 copy.38
  2.5 0.9 fusion.14
  3.4 0.2 broadcast_add_fusion
  3.7 0.1 copy.35
  3.8 0.4 fusion.16
  4.2 1.4 scatter_custom_fusion
  5.6 1.2 concatenate.3
  6.9 4.2 gather_fusion
  11.1 6.3 %all-to-all-start = ((bf16[8,64,3584]{2,1,0:T(8,128)(2,1)}), bf16[8,64,3584]{2,1,0:T(8,128)(2,1)}, u32[]{:S(2)}, u32[]{:S(2)}) async-start(bf16[8,64,3584]{2,1,0:T(8,128)(2,1)} %bitcast.60), calls=%async_computation | async-start | bytes 7340032 | tf_op jit(solution)/shard_map/all_to_all | solution.py:37
  17.4 14.5 %copy.50 = bf16[448,8,16,128]{3,2,1,0:T(8,128)(2,1)} copy(bf16[448,8,16,128]{3,1,2,0:T(8,128)(2,1)} %bitcast.61) | data formatting | bytes 29360128
  31.9 0.0 copy-start.2
  31.9 68.3 %all-to-all-done = bf16[8,64,3584]{2,1,0:T(8,128)(2,1)} async-done(((bf16[8,64,3584]{2,1,0:T(8,128)(2,1)}), bf16[8,64,3584]{2,1,0:T(8,128)(2,1)}, u32[]{:S(2)}, u32[]{:S(2)}) %all-to-all-start) | async-done | bytes 3670048 | tf_op jit(solution)/shard_map/all_to_all | solution.py:37
  100.3 4.1 copy.40
  104.3 0.0 copy-done.2
  104.3 13.2 %fusion.11 = bf16[16,8,4,128]{3,1,2,0:T(8,128)(2,1)S(1)} fusion(bf16[8,16,4,3584]{3,0,2,1:T(8,128)(2,1)S(1)} %bitcast.63, bf16[3584,16,128,1]{2,1,0,3:T(8,128)(2,1)} %bitcast.62, f32[16,128]{1,0:T(8,128)S(1)} %bitcast.70), kind=kOutput, calls=%fused_computation.16 | convolution fusion | flops 469958656 | bytes 18489344 | tf_op jit(solution)/shard_map/sbcd,dbe->sbce/dot_general | solution.py:40
  117.6 10.2 %all_gather.3 = bf16[4,8,64,128]{3,2,1,0:T(8,128)(2,1)S(1)} all-gather(bf16[1,8,64,128]{3,2,1,0:T(8,128)(2,1)S(1)} %copy.42), channel_id=1, replica_groups=mesh['layer'=4,'tok'=8] {'layer'}, dimensions={0}, use_global_device_ids=true | all-gather | bytes 655360 | tf_op jit(solution)/shard_map/all_gather | solution.py:47
  127.8 0.6 gather_fusion.1
  128.5 25.9 %convolution_convert_fusion = bf16[4,16,8,4,3584]{4,2,3,1,0:T(8,128)(2,1)} fusion(bf16[4,16,128,3584,1]{3,2,4,1,0:T(8,128)(2,1)} %bitcast.59, bf16[4,8,16,4,128]{4,3,2,1,0:T(4,128)(2,1)S(1)} %bitcast.64, pred[4]{0:T(512)(128)(4,1)S(1)} %get-tuple-element.3, bf16[4]{0:T(256)(128)(2,1)S(1)} %get-tuple-element.2), kind=kOutput, calls=%fused_computation.7 | convolution fusion | flops 1886912512 | bytes 73924624 | tf_op jit(solution)/shard_map/snbce,sbed->snbcd/dot_general | solution.py:57
  154.4 15.6 %copy.44 = bf16[4,8,64,3584]{3,2,0,1:T(8,128)(2,1)} copy(bf16[4,8,64,3584]{3,1,2,0:T(8,128)(2,1)} %bitcast.58) | data formatting | bytes 29360128 | tf_op jit(solution)/shard_map/reshape | solution.py:64
  170.0 0.0 copy-start.1
  170.0 5.7 all-to-all-start.1
  175.7 0.6 gather_fusion.2
  176.2 0.1 fusion.27
  176.3 0.0 copy-done.1
  176.4 318.0 %all-to-all-done.1 = bf16[4,8,64,3584]{3,2,0,1:T(8,128)(2,1)} async-done(((bf16[4,8,64,3584]{3,2,0,1:T(8,128)(2,1)}), bf16[4,8,64,3584]{3,2,0,1:T(8,128)(2,1)}, u32[]{:S(2)}, u32[]{:S(2)}) %all-to-all-start.1) | async-done | bytes 14680096 | tf_op jit(solution)/shard_map/all_to_all | solution.py:66
  494.4 13.4 %copy.45 = bf16[4,8,64,3584]{3,2,1,0:T(8,128)(2,1)} copy(bf16[4,8,64,3584]{3,2,0,1:T(8,128)(2,1)} %all-to-all-done.1) | data formatting | bytes 29360128 | tf_op jit(solution)/shard_map/all_to_all | solution.py:66
  507.8 32.0 %gather_fusion.3 = bf16[1024,3584]{1,0:T(8,128)(2,1)} fusion(bf16[4,512,3584]{2,1,0:T(8,128)(2,1)} %bitcast.56, s32[1024]{0:T(1024)S(1)} %bitcast.57), kind=kCustom, calls=%fused_computation.3 | custom fusion | bytes 14688256 | tf_op jit(solution)/shard_map/vmap()/gather | solution.py:70
  539.8 16.2 %reshape.172 = f32[4,128,2,3584]{3,2,1,0:T(2,128)} reshape(bf16[1024,3584]{1,0:T(8,128)(2,1)} %gather_fusion.3) | data formatting | bytes 22020096 | tf_op jit(solution)/shard_map/convert_element_type | solution.py:71
  556.0 22.3 %reduce_sum.39 = f32[4,128,3584]{2,1,0:T(8,128)} reduce(f32[4,128,2,3584]{3,2,1,0:T(2,128)} %reshape.172, f32[]{:T(128)} %constant.75.clone.1), dimensions={2}, to_apply=%region_4.5 | reduce | flops 1835008 | bytes 22020100 | tf_op jit(solution)/shard_map/reduce_sum | solution.py:71
  578.3 0.0 copy-start
  578.3 4.3 multiply_reduce_fusion
  582.6 1.0 fusion.4
  583.6 0.0 copy-done
  583.6 0.4 fusion.3
  584.0 0.5 multiply_bitcast_fusion
  (16 shorter events, 0.2 us)
Async XLA Ops:
  11.1 89.2 %all-to-all-start = ((bf16[8,64,3584]{2,1,0:T(8,128)(2,1)}), bf16[8,64,3584]{2,1,0:T(8,128)(2,1)}, u32[]{:S(2)}, u32[]{:S(2)}) async-start(bf16[8,64,3584]{2,1,0:T(8,128)(2,1)} %bitcast.60), calls=%async_computation | async-start | bytes 7340032 | tf_op jit(solution)/shard_map/all_to_all | solution.py:37
  31.9 72.4 %copy-start.2 = (f32[1,2048]{1,0:T(1,128)S(1)}, f32[1,2048]{1,0:T(1,128)}, u32[]{:S(2)}) copy-start(f32[1,2048]{1,0:T(1,128)} %param.11) | copy-start | bytes 24580
  170.0 6.3 %copy-start.1 = (f32[1,3584]{1,0:T(1,128)S(1)}, f32[1,3584]{1,0:T(1,128)}, u32[]{:S(2)}) copy-start(f32[1,3584]{1,0:T(1,128)} %param.13) | copy-start | bytes 43012
  170.0 324.4 %all-to-all-start.1 = ((bf16[4,8,64,3584]{3,2,0,1:T(8,128)(2,1)}), bf16[4,8,64,3584]{3,2,0,1:T(8,128)(2,1)}, u32[]{:S(2)}, u32[]{:S(2)}) async-start(bf16[4,8,64,3584]{3,2,0,1:T(8,128)(2,1)} %copy.44), calls=%async_computation.1 | async-start | bytes 29360128 | tf_op jit(solution)/shard_map/all_to_all | solution.py:66
  578.3 5.3 copy-start
where the time goes:
time: 586 us; the launch traced here: 585 us
  waiting for transfers between devices  386 us (66%)
  local copies, waits for them, and re-layouts  106 us (18%)
  matrix products  39.1 us (7%)
  other arithmetic  30.2 us (5%)
  starting transfers between devices  12 us (2%)
  blocking collectives  10.2 us (2%)
    all_to_all x1, waiting for transfers between devices, body(): lax.all_to_all(terms, 'tok', split_axis=1, concat_axis=1, tiled=True)  318 us
    all_to_all x1, waiting for transfers between devices, body(): lax.all_to_all(outgoing, 'tok', split_axis=0, concat_axis=0, tiled=True)  68.3 us
    gather x1, local copies, waits for them, and re-layouts, body(): rows[where_at]  32 us
    dot_general x1, matrix products, body(): jnp.einsum('snbce,sbed->snbcd', chosen_codes.reshape(slot_sets, tok_count...  25.9 us
    reduce_sum x1, other arithmetic, body(): jnp.sum(picked.astype(jnp.float32).reshape(slot_sets, tok_rows, topk, wid...  22.3 us
    convert_element_type x1, local copies, waits for them, and re-layouts, body(): picked.astype(jnp.float32).reshape(slot_sets, tok_rows, topk, width)  16.2 us
    reshape x1, local copies, waits for them, and re-layouts, body(): terms = jnp.einsum('snbce,sbed->snbcd', chosen_codes.reshape(slot_sets, t...  15.6 us
    unnamed x9, local copies, waits for them, and re-layouts  15.3 us
  transfers between devices with their start and end apart: 2, of which 2 were waited for; matrix products, arithmetic and copies ran while one was open for 3% of the time, Pallas kernels for 0%

commit v1 on v0

--- a/solution.py
+++ b/solution.py
@@ -63,9 +63,10 @@
         .astype(jnp.bfloat16)
         .reshape(slot_sets, tok_count, per_owner * capacity, width)
     )
-    returned = lax.all_to_all(terms, "tok", split_axis=1, concat_axis=1, tiled=True).reshape(
-        slot_sets, slot_count, width
-    )
+    returned = jnp.concatenate(
+        lax.all_to_all(jnp.stack(jnp.split(terms, lax.axis_size("tok"), axis=1)), "tok", 0, 0),
+        axis=1,
+    ).reshape(slot_sets, slot_count, width)
     source_positions = jnp.take(positions, sources, axis=0)
     picked = jax.vmap(lambda rows, where_at: rows[where_at])(returned, source_positions)
     parts = jnp.sum(picked.astype(jnp.float32).reshape(slot_sets, tok_rows, topk, width), axis=2)

time: 586 us -> 635 us (1.084)
  local copies, waits for them, and re-layouts: 106 us -> 155 us
    split x0 -> x1, local copies, waits for them, and re-layouts: none -> 48.9 us  [body(): jnp.split(terms, lax.axis_size('tok'), axis=1)]
    unnamed x9 -> x28, local copies, waits for them, and re-layouts: 15.3 us -> 30.6 us
    all_to_all x1 -> x0, local copies, waits for them, and re-layouts: 13.4 us -> none  [body(): lax.all_to_all(terms, 'tok', split_axis=1, concat_axis=1, tiled=True)]
  transfers between devices with their start and end apart: 2 -> 2, of which waited for: 2 -> 2; matrix products, arithmetic and copies ran while one was open for 3% -> 2% of each run, Pallas kernels for 0% -> 0%
where the time goes in v1:
time: 635 us; the launch traced here: 633 us
  waiting for transfers between devices  386 us (61%)
  local copies, waits for them, and re-layouts  155 us (24%)
  matrix products  39.2 us (6%)
  other arithmetic  30.2 us (5%)
  starting transfers between devices  12.2 us (2%)
  blocking collectives  10.2 us (2%)
    all_to_all x1, waiting for transfers between devices, body(): lax.all_to_all(jnp.stack(jnp.split(terms, lax.axis_size('tok'), axis=1)),...  318 us
    all_to_all x1, waiting for transfers between devices, body(): lax.all_to_all(outgoing, 'tok', split_axis=0, concat_axis=0, tiled=True)  68.3 us
    split x1, local copies, waits for them, and re-layouts, body(): jnp.split(terms, lax.axis_size('tok'), axis=1)  48.9 us
    gather x1, local copies, waits for them, and re-layouts, body(): rows[where_at]  31.9 us
    unnamed x28, local copies, waits for them, and re-layouts  30.6 us
    dot_general x1, matrix products, body(): jnp.einsum('snbce,sbed->snbcd', chosen_codes.reshape(slot_sets, tok_count...  25.9 us
    reduce_sum x1, other arithmetic, body(): jnp.sum(picked.astype(jnp.float32).reshape(slot_sets, tok_rows, topk, wid...  22.3 us
    convert_element_type x1, local copies, waits for them, and re-layouts, body(): picked.astype(jnp.float32).reshape(slot_sets, tok_rows, topk, width)  16.2 us
  transfers between devices with their start and end apart: 2, of which 2 were waited for; matrix products, arithmetic and copies ran while one was open for 2% of the time, Pallas kernels for 0%

profile of v1, /device:TPU:0, one launch (start us, length us, event | category | flops | bytes accessed | tf_op | source)
XLA Modules:
  0.0 633.4 jit_solution(7401362681930557928)
XLA Ops:
  0.6 0.0 copy-start.5
  0.7 0.9 copy.56
  1.6 1.0 copy.60
  2.6 0.9 fusion.22
  3.5 0.2 broadcast_add_fusion
  3.8 0.1 copy.57
  3.8 0.4 fusion.24
  4.3 1.4 scatter_custom_fusion
  5.7 0.0 copy-done.5
  5.7 0.1 concatenate.3
  5.8 4.2 gather_fusion
  10.0 6.3 all-to-all-start
  16.3 14.5 %copy.87 = bf16[448,8,16,128]{3,2,1,0:T(8,128)(2,1)} copy(bf16[448,8,16,128]{3,1,2,0:T(8,128)(2,1)} %bitcast.94) | data formatting | bytes 29360128
  30.8 0.0 copy-start.8
  30.9 68.3 %all-to-all-done = bf16[8,64,3584]{2,1,0:T(8,128)(2,1)} async-done(((bf16[8,64,3584]{2,1,0:T(8,128)(2,1)}), bf16[8,64,3584]{2,1,0:T(8,128)(2,1)}, u32[]{:S(2)}, u32[]{:S(2)}) %all-to-all-start) | async-done | bytes 3670048 | tf_op jit(solution)/shard_map/all_to_all | solution.py:37
  99.2 4.1 copy.62
  103.3 0.0 copy-done.8
  103.3 13.2 %fusion.19 = bf16[16,8,4,128]{3,1,2,0:T(8,128)(2,1)S(1)} fusion(bf16[8,16,4,3584]{3,0,2,1:T(8,128)(2,1)S(1)} %bitcast.96, bf16[3584,16,128,1]{2,1,0,3:T(8,128)(2,1)} %bitcast.95, f32[16,128]{1,0:T(8,128)S(1)} %bitcast.103), kind=kOutput, calls=%fused_computation.32 | convolution fusion | flops 469958656 | bytes 18489344 | tf_op jit(solution)/shard_map/sbcd,dbe->sbce/dot_general | solution.py:40
  116.5 10.2 %all_gather.3 = bf16[4,8,64,128]{3,2,1,0:T(8,128)(2,1)S(1)} all-gather(bf16[1,8,64,128]{3,2,1,0:T(8,128)(2,1)S(1)} %copy.64), channel_id=1, replica_groups=mesh['layer'=4,'tok'=8] {'layer'}, dimensions={0}, use_global_device_ids=true | all-gather | bytes 655360 | tf_op jit(solution)/shard_map/all_gather | solution.py:47
  126.7 0.6 gather_fusion.1
  127.4 25.9 %convolution_convert_fusion = bf16[4,16,8,4,3584]{4,2,3,1,0:T(8,128)(2,1)} fusion(bf16[4,16,128,3584,1]{3,2,4,1,0:T(8,128)(2,1)} %bitcast.92, bf16[4,8,16,4,128]{4,3,2,1,0:T(4,128)(2,1)S(1)} %bitcast.97, pred[4]{0:T(512)(128)(4,1)S(1)} %get-tuple-element.11, bf16[4]{0:T(256)(128)(2,1)S(1)} %get-tuple-element.10), kind=kOutput, calls=%fused_computation.7 | convolution fusion | flops 1886912512 | bytes 73924624 | tf_op jit(solution)/shard_map/snbce,sbed->snbcd/dot_general | solution.py:57
  153.3 48.9 %fusion.39 = (bf16[4,1,64,3584]{3,1,2,0:T(2,128)(2,1)S(1)}, bf16[4,1,64,3584]{3,1,2,0:T(2,128)(2,1)S(1)}, bf16[4,1,64,3584]{3,1,2,0:T(2,128)(2,1)}, bf16[4,1,64,...) fusion(bf16[4,8,64,3584]{3,1,2,0:T(8,128)(2,1)} %bitcast.90), kind=kLoop, calls=%fused_computation.70 | loop fusion | bytes 29360128 | tf_op jit(solution)/shard_map/split | solution.py:67
  202.3 0.0 copy-start.4
  202.3 3.7 fusion.9
  206.0 0.0 copy-start.3
  206.0 0.0 copy-done.4
  206.0 1.5 fusion.8
  207.4 0.0 copy-start.2
  207.4 1.2 copy-done.3
  208.7 1.5 fusion.7
  210.2 0.0 copy-start.1
  210.2 0.0 copy-done.2
  210.2 1.5 fusion.6
  211.7 0.0 copy-start
  211.7 1.2 copy-done.1
  212.9 1.6 fusion.5
  214.4 0.0 copy-done
  214.4 1.5 fusion.4
  215.9 1.5 fusion.3
  217.4 1.5 fusion.2
  218.9 0.0 copy-start.7
  218.9 5.9 all-to-all-start.1
  224.8 0.6 gather_fusion.2
  225.4 0.1 fusion.35
  225.5 0.0 copy-done.7
  225.5 317.8 %all-to-all-done.1 = bf16[8,4,1,64,3584]{4,3,1,2,0:T(8,128)(2,1)} async-done(((bf16[8,4,1,64,3584]{4,3,1,2,0:T(8,128)(2,1)}), bf16[8,4,1,64,3584]{4,3,1,2,0:T(8,128)(2,1)}, u32[]{:S(2)}, u32[]{:S(2)}) %all-to-all-start.1) | async-done | bytes 14680096 | tf_op jit(solution)/shard_map/all_to_all | solution.py:67
  543.3 13.5 %copy.74 = bf16[4,8,1,64,3584]{4,3,1,0,2:T(8,128)(2,1)} copy(bf16[4,8,1,64,3584]{4,3,0,2,1:T(8,128)(2,1)} %bitcast.29) | data formatting | bytes 29360128 | tf_op jit(solution)/shard_map/reshape | solution.py:66
  556.8 31.9 %gather_fusion.3 = bf16[1024,3584]{1,0:T(8,128)(2,1)} fusion(bf16[4,512,3584]{2,1,0:T(8,128)(2,1)} %bitcast.89, s32[1024]{0:T(1024)S(1)} %bitcast.91), kind=kCustom, calls=%fused_computation.3 | custom fusion | bytes 14688256 | tf_op jit(solution)/shard_map/vmap()/gather | solution.py:71
  588.7 16.2 %reshape.172 = f32[4,128,2,3584]{3,2,1,0:T(2,128)} reshape(bf16[1024,3584]{1,0:T(8,128)(2,1)} %gather_fusion.3) | data formatting | bytes 22020096 | tf_op jit(solution)/shard_map/convert_element_type | solution.py:72
  604.8 22.3 %reduce_sum.39 = f32[4,128,3584]{2,1,0:T(8,128)} reduce(f32[4,128,2,3584]{3,2,1,0:T(2,128)} %reshape.172, f32[]{:T(128)} %constant.75.clone.1), dimensions={2}, to_apply=%region_4.5 | reduce | flops 1835008 | bytes 22020100 | tf_op jit(solution)/shard_map/reduce_sum | solution.py:72
  627.2 0.0 copy-start.6
  627.2 4.3 multiply_reduce_fusion
  631.4 1.0 fusion.12
  632.5 0.0 copy-done.6
  632.5 0.4 fusion.11
  632.9 0.5 multiply_bitcast_fusion
  (16 shorter events, 0.2 us)
Async XLA Ops:
  0.6 5.1 copy-start.5
  10.0 89.2 %all-to-all-start = ((bf16[8,64,3584]{2,1,0:T(8,128)(2,1)}), bf16[8,64,3584]{2,1,0:T(8,128)(2,1)}, u32[]{:S(2)}, u32[]{:S(2)}) async-start(bf16[8,64,3584]{2,1,0:T(8,128)(2,1)} %bitcast.93), calls=%async_computation | async-start | bytes 7340032 | tf_op jit(solution)/shard_map/all_to_all | solution.py:37
  30.8 72.4 %copy-start.8 = (f32[1,2048]{1,0:T(1,128)S(1)}, f32[1,2048]{1,0:T(1,128)}, u32[]{:S(2)}) copy-start(f32[1,2048]{1,0:T(1,128)} %param.11) | copy-start | bytes 24580
  202.3 3.7 copy-start.4
  206.0 2.7 copy-start.3
  207.4 2.7 copy-start.2
  210.2 2.7 copy-start.1
  211.7 2.7 copy-start
  218.9 6.6 %copy-start.7 = (f32[1,3584]{1,0:T(1,128)S(1)}, f32[1,3584]{1,0:T(1,128)}, u32[]{:S(2)}) copy-start(f32[1,3584]{1,0:T(1,128)} %param.13) | copy-start | bytes 43012
  218.9 324.4 %all-to-all-start.1 = ((bf16[8,4,1,64,3584]{4,3,1,2,0:T(8,128)(2,1)}), bf16[8,4,1,64,3584]{4,3,1,2,0:T(8,128)(2,1)}, u32[]{:S(2)}, u32[]{:S(2)}) async-start(bf16[8,4,1,64,3584]{4,3,1,2,0:T(8,128)(2,1)} %fusion.2), calls=%async_computation.1 | async-start | bytes 29360128 | tf_op jit(solution)/shard_map/all_to_all | solution.py:67
  627.2 5.3 copy-start.6
